TPU v7x, 32 devices: a whole 2x2x4 slice. The times are simulated.
32 devices in a mesh: groups: 1, gx: 32 (over z, y, x, core).
Axes of the slice: x: 2, y: 2, z: 4, core: 2. Of those that a mesh axis runs over, the one named last changes fastest.
Arguments:
- solid_state: float32 [9, 2, 1, 256, 4, 128], P(None, None, 'groups', 'gx'), may hold values from -6 to 6
- water_state: float32 [4, 2, 1, 128, 12, 256], P(None, None, 'groups', 'gx'), may hold values from -6 to 6
- lame_lambda: float32 [256, 4, 128], P('gx'), may hold values from 0.4 to 1.2
- shear_mu: float32 [256, 4, 128], P('gx'), may hold values from 0.1 to 0.5
- solid_buoy: float32 [256, 4, 128], P('gx'), may hold values from 0.4 to 1
- water_kappa: float32 [128, 12, 256], P('gx'), may hold values from 0.5 to 1
- water_buoy: float32 [128, 12, 256], P('gx'), may hold values from 0.6 to 1.2
- seafloor: int32 [128, 256], P('gx'), may hold values from 6 to 12
- source_cell: int32 [1], P('groups'), may hold values from 0 to 196607
- wavelet: float32 [4, 1], P(None, 'groups'), may hold values from -48 to 48
- receiver_column: int32 [128], replicated, may hold values from 0 to 32767
- observed: float32 [4, 1, 128], P(None, 'groups'), may hold values from -6 to 6
Outputs:
- grad_lambda: float32 [256, 4, 128], P('gx', 'groups')
- grad_mu: float32 [256, 4, 128], P('gx', 'groups')
- grad_kappa: float32 [128, 12, 256], P('gx', 'groups')
- residuals: float32 [4, 1, 128], P(None, 'groups')
Inputs may be any that keep to these rules, and one draw needn't show every extreme that they name: Every column holds water from z = 0 to z = seafloor - 1 and rock below it. source_cell is (z * 128 + y) * 256 + x of a water cell with z below 6. receiver_column is y * 256 + x; two nodes may share a column.
All inputs are finite; a program needn't handle non-finite values.
Results may differ from a plain program's by a relative error of at most 0.00014.
Values sent between devices are 32-bit elements; how exact they have to be, the bound alone decides.
No kernel may reach another device: no remote copies, remote signals or barrier semaphores. Data moves between devices by JAX's collectives and lax.ppermute only.
A program may use at most 64 MiB of HBM per device.

v0:
```python
import jax
import jax.numpy as jnp
from jax import lax
from jax.sharding import PartitionSpec as P

COEFF = (1225.0 / 1024.0, -245.0 / 3072.0, 49.0 / 5120.0, -5.0 / 7168.0)
TIME_STEP = 0.2


def with_halo(array, sides, width):
    for axis, dim in sides:
        devices, length = (lax.axis_size(axis), array.shape[dim])
        up = [(i, (i + 1) % devices) for i in range(devices - 1)]
        down = [(j, i) for i, j in up]
        last = lax.slice_in_dim(array, length - width, length, axis=dim)
        first = lax.slice_in_dim(array, 0, width, axis=dim)
        before = lax.ppermute(last, axis, up)
        after = lax.ppermute(first, axis, down)
        array = jnp.concatenate([before, array, after], axis=dim)
    return array


def stencil(padded, axis, forward):
    length = padded.shape[axis] - 8
    summed = None
    for offset in range(1, 5):
        if forward:
            front_at, back_at = (4 + offset, 5 - offset)
        else:
            front_at, back_at = (3 + offset, 4 - offset)
        front = lax.slice_in_dim(padded, front_at, front_at + length, axis=axis)
        back = lax.slice_in_dim(padded, back_at, back_at + length, axis=axis)
        addend = COEFF[offset - 1] * (front - back)
        summed = addend if summed is None else summed + addend
    return summed


def padded_zero(field, axis):
    widths = [(0, 0)] * field.ndim
    widths[axis] = (4, 4)
    return jnp.pad(field, widths)


def derive(field, axis, forward):
    return stencil(padded_zero(field, axis), axis, forward)


def on_device(
    solid_state,
    water_state,
    lame_lambda,
    shear_mu,
    solid_buoy,
    water_kappa,
    water_buoy,
    seafloor,
    source_cell,
    wavelet,
    receiver_column,
    observed,
):
    parts = lax.axis_size("gx")
    place = lax.axis_index("gx")
    width_x = solid_state.shape[3]
    total_y = solid_state.shape[5]
    total_x = width_x * parts
    shots = solid_state.shape[2]
    shard_axis = 2
    anchor_y = place * water_state.shape[3]
    anchor_x = 0

    def water_halo(field):
        return with_halo(field, (("gx", 2),), 4)

    def water_derive(field, axis, forward):
        if axis == shard_axis:
            return stencil(water_halo(field), axis, forward)
        return derive(field, axis, forward)

    def solid_halo(stacked):
        return with_halo(stacked, (("gx", 3),), 4)

    vel_x, vel_y, vel_z = (solid_state[0], solid_state[1], solid_state[2])
    sig_xx, sig_yy, sig_zz = (solid_state[3], solid_state[4], solid_state[5])
    sig_xy, sig_xz, sig_yz = (solid_state[6], solid_state[7], solid_state[8])
    pressure, flow_x, flow_y, flow_z = (
        water_state[0],
        water_state[1],
        water_state[2],
        water_state[3],
    )
    local_y = pressure.shape[2]
    depth_rows = pressure.shape[3]
    local_x = pressure.shape[4]
    depth_idx = lax.broadcasted_iota(jnp.int32, (1, depth_rows, 1), 1)
    floor_rows = seafloor[:, None, :]
    live = (depth_idx < floor_rows).astype(jnp.float32)
    bottom = (depth_idx == floor_rows - 1).astype(jnp.float32)
    above = (depth_idx < floor_rows - 1).astype(jnp.float32)
    rows_y = lax.broadcasted_iota(jnp.int32, (local_y, 1, 1), 0) + anchor_y
    cols_x = lax.broadcasted_iota(jnp.int32, (1, 1, local_x), 2) + anchor_x
    flat_cell = (depth_idx * total_y + rows_y) * total_x + cols_x
    source_hot = (flat_cell[None] == source_cell[:, None, None, None]).astype(jnp.float32)
    node_y = receiver_column // total_x
    node_x = receiver_column % total_x
    inside = (
        (node_y >= anchor_y)
        & (node_y < anchor_y + local_y)
        & (node_x >= anchor_x)
        & (node_x < anchor_x + local_x)
    )
    local_col = (node_y - anchor_y) * local_x + (node_x - anchor_x)
    column_iota = lax.broadcasted_iota(jnp.int32, (1, local_y * local_x), 1)
    node_hot = ((column_iota == local_col[:, None]) & inside[:, None]).astype(jnp.float32)
    grad_lambda = jnp.zeros(lame_lambda.shape, jnp.float32)
    grad_mu = jnp.zeros(lame_lambda.shape, jnp.float32)
    grad_kappa = jnp.zeros(water_kappa.shape, jnp.float32)
    misfits = []
    for step in range(wavelet.shape[0]):
        floor_pressure = jnp.sum(pressure * bottom, axis=3)
        stress_pad = solid_halo(jnp.stack([sig_xx, sig_xy, sig_xz]))
        vel_x = vel_x + TIME_STEP * solid_buoy * (
            stencil(stress_pad[0], 2, True) + derive(sig_xy, 4, False) + derive(sig_xz, 3, False)
        )
        vel_y = vel_y + TIME_STEP * solid_buoy * (
            stencil(stress_pad[1], 2, False) + derive(sig_yy, 4, True) + derive(sig_yz, 3, False)
        )
        vel_z = vel_z + TIME_STEP * solid_buoy * (
            stencil(stress_pad[2], 2, False) + derive(sig_yz, 4, False) + derive(sig_zz, 3, True)
        )
        floor_velocity = lax.all_to_all(
            jnp.transpose(vel_z[:, :, :, 0, :], (0, 1, 3, 2)),
            "gx",
            split_axis=2,
            concat_axis=3,
            tiled=True,
        )
        flow_x = (flow_x - TIME_STEP * water_buoy * water_derive(pressure, 4, True)) * live
        flow_y = (flow_y - TIME_STEP * water_buoy * water_derive(pressure, 2, True)) * live
        flow_z = (
            flow_z - TIME_STEP * water_buoy * derive(pressure, 3, True)
        ) * above + floor_velocity[:, :, :, None, :] * bottom
        velocity_pad = solid_halo(jnp.stack([vel_x, vel_y, vel_z]))
        strain_x = stencil(velocity_pad[0], 2, False)
        strain_y = derive(vel_y, 4, False)
        strain_z = derive(vel_z, 3, False)
        dilation = strain_x + strain_y + strain_z
        shear_xy = derive(vel_x, 4, True) + stencil(velocity_pad[1], 2, True)
        shear_xz = derive(vel_x, 3, True) + stencil(velocity_pad[2], 2, True)
        shear_yz = derive(vel_y, 3, True) + derive(vel_z, 4, True)
        lam_part = lame_lambda * dilation
        sig_xx = sig_xx + TIME_STEP * (lam_part + 2.0 * shear_mu * strain_x)
        sig_yy = sig_yy + TIME_STEP * (lam_part + 2.0 * shear_mu * strain_y)
        sig_zz = sig_zz + TIME_STEP * (lam_part + 2.0 * shear_mu * strain_z)
        sig_xy = sig_xy + TIME_STEP * shear_mu * shear_xy
        sig_xz = sig_xz + TIME_STEP * shear_mu * shear_xz
        sig_yz = sig_yz + TIME_STEP * shear_mu * shear_yz
        rock_pressure = jnp.transpose(
            lax.all_to_all(floor_pressure, "gx", split_axis=3, concat_axis=2, tiled=True),
            (0, 1, 3, 2),
        )
        sig_zz = sig_zz.at[:, :, :, 0, :].set(-rock_pressure)
        grad_lambda = grad_lambda + jnp.sum(dilation[0] * dilation[1], axis=0)
        normal_part = (
            strain_x[0] * strain_x[1] + strain_y[0] * strain_y[1] + strain_z[0] * strain_z[1]
        )
        shear_part = (
            shear_xy[0] * shear_xy[1] + shear_xz[0] * shear_xz[1] + shear_yz[0] * shear_yz[1]
        )
        grad_mu = grad_mu + jnp.sum(2.0 * normal_part + shear_part, axis=0)
        pressure = (
            pressure
            - TIME_STEP
            * water_kappa
            * (
                water_derive(flow_x, 4, False)
                + water_derive(flow_y, 2, False)
                + derive(flow_z, 3, False)
            )
        ) * live
        pressure = pressure.at[0].add(wavelet[step][:, None, None, None] * source_hot)
        surface = jnp.sum(pressure * bottom, axis=3)
        partial_record = jnp.einsum(
            "sc,rc->sr",
            surface[0].reshape(shots, local_y * local_x),
            node_hot,
            precision=lax.Precision.HIGHEST,
        )
        recorded = lax.psum(partial_record, "gx")
        misfit = recorded - observed[step]
        scaled = misfit * lax.rsqrt(jnp.mean(misfit * misfit, axis=1, keepdims=True) + 1e-06)
        inject = jnp.dot(
            scaled, node_hot, precision=lax.Precision.HIGHEST, preferred_element_type=jnp.float32
        ).reshape(shots, local_y, local_x)
        pressure = pressure.at[1].add(inject[:, :, None, :] * bottom)
        grad_kappa = grad_kappa + jnp.sum(pressure[0] * pressure[1], axis=0)
        misfits.append(misfit)
    return (grad_lambda, grad_mu, grad_kappa, jnp.stack(misfits))


def solution(mesh):
    placed = (
        P(None, None, "groups", "gx", None, None),
        P(None, None, "groups", "gx", None, None),
        P("gx", None, None),
        P("gx", None, None),
        P("gx", None, None),
        P("gx", None, None),
        P("gx", None, None),
        P("gx", None),
        P("groups"),
        P(None, "groups"),
        P(),
        P(None, "groups", None),
    )
    return jax.shard_map(
        on_device,
        mesh=mesh,
        in_specs=placed,
        out_specs=(
            P("gx", "groups", None),
            P("gx", "groups", None),
            P("gx", "groups", None),
            P(None, "groups", None),
        ),
        check_vma=False,
    )
```

profile of v0, /device:TPU:0, one launch (start us, length us, event | category | flops | bytes accessed | tf_op | source)
XLA Modules:
  0.0 367.0 jit_solution(11349562170741559003)
XLA Ops:
  2.9 3.0 collective-permute-start.11
  6.8 1.3 collective-permute-start.1
  8.1 5.1 %collective-permute-start = (f32[3,2,1,4,4,128]{5,4,3,2,1,0:T(4,128)S(1)}, f32[3,2,1,4,4,128]{5,4,3,2,1,0:T(4,128)S(1)}, u32[]{:S(2)}, u32[]{:S(2)}) collective-permute-start(f32[3,2,1,4,4,128]{5,4,3,2,1,0:T(4,128)S(1)} %get-tuple-element.248), channel_id=1, source_target_pairs={{0,1},{1,2},{2,3},{3,4},{4,5},{5,6},{6,7},{7,8},{8,9},{9,10},{10,1... | collective-permute-start | bytes 147464 | tf_op jit(solution)/shard_map/ppermute | solution.py:17
  19.5 9.7 %all-to-all-start.1 = ((f32[2,1,128,8]{3,0,1,2:T(2,128)}), f32[2,1,128,8]{3,0,1,2:T(2,128)S(1)}, u32[]{:S(2)}, u32[]{:S(2)}) async-start(f32[2,1,128,8]{3,0,1,2:T(2,128)} %copy.963), calls=%async_computation.1 | async-start | bytes 262144 | tf_op jit(solution)/shard_map/all_to_all | solution.py:131
  29.7 1.4 collective-permute-start.3
  31.2 3.0 collective-permute-start.2
  34.2 3.3 all-to-all-done.1
  39.1 1.3 collective-permute-start.5
  40.4 3.0 collective-permute-start.4
  43.9 3.4 collective-permute-start.12
  47.3 1.3 collective-permute-start.13
  49.1 1.4 collective-permute-done.13
  52.6 12.4 %all-to-all-start = ((f32[2,1,4,256]{2,0,1,3:T(2,128)}), f32[2,1,4,256]{2,0,1,3:T(2,128)S(1)}, u32[]{:S(2)}, u32[]{:S(2)}) async-start(f32[2,1,4,256]{2,0,1,3:T(2,128)} %copy.948), calls=%async_computation | async-start | bytes 524288 | tf_op jit(solution)/shard_map/all_to_all | solution.py:159
  65.5 40.5 %psum.28 = f32[1,128]{1,0:T(1,128)S(1)} all-reduce(f32[1,128]{1,0:T(1,128)S(1)} %fusion.7), channel_id=1, replica_groups=mesh['groups'=1,'gx'=32] {'gx'}, use_global_device_ids=true, to_apply=%region_2.3 | all-reduce | flops 128 | bytes 1024 | tf_op jit(solution)/shard_map/psum | solution.py:189
  107.8 1.3 collective-permute-start.18
  109.1 3.0 collective-permute-start.19
  113.6 6.2 %all-to-all-start.3 = ((f32[2,1,128,8]{3,0,1,2:T(2,128)}), f32[2,1,128,8]{3,0,1,2:T(2,128)S(1)}, u32[]{:S(2)}, u32[]{:S(2)}) async-start(f32[2,1,128,8]{3,0,1,2:T(2,128)} %copy.978), calls=%async_computation.3 | async-start | bytes 262144 | tf_op jit(solution)/shard_map/all_to_all | solution.py:131
  119.9 1.3 collective-permute-start.7
  121.2 3.0 collective-permute-start.6
  124.2 3.8 %all-to-all-done.3 = f32[2,1,128,8]{3,0,1,2:T(2,128)S(1)} async-done(((f32[2,1,128,8]{3,0,1,2:T(2,128)}), f32[2,1,128,8]{3,0,1,2:T(2,128)S(1)}, u32[]{:S(2)}, u32[]{:S(2)}) %all-to-all-start.3) | async-done | bytes 8224 | tf_op jit(solution)/shard_map/all_to_all | solution.py:131
  129.1 1.3 collective-permute-start.9
  130.4 3.0 collective-permute-start.8
  133.9 3.4 collective-permute-start.20
  137.3 1.3 collective-permute-start.21
  139.1 1.4 collective-permute-done.21
  142.7 11.9 %all-to-all-start.2 = ((f32[2,1,4,256]{2,0,1,3:T(2,128)}), f32[2,1,4,256]{2,0,1,3:T(2,128)S(1)}, u32[]{:S(2)}, u32[]{:S(2)}) async-start(f32[2,1,4,256]{2,0,1,3:T(2,128)} %copy.966), calls=%async_computation.2 | async-start | bytes 524288 | tf_op jit(solution)/shard_map/all_to_all | solution.py:159
  155.0 40.5 %psum.29 = f32[1,128]{1,0:T(1,128)S(1)} all-reduce(f32[1,128]{1,0:T(1,128)S(1)} %fusion.5), channel_id=1, replica_groups=mesh['groups'=1,'gx'=32] {'gx'}, use_global_device_ids=true, to_apply=%region_6.7 | all-reduce | flops 128 | bytes 1024 | tf_op jit(solution)/shard_map/psum | solution.py:189
  198.6 3.0 collective-permute-start.25
  203.1 6.2 %all-to-all-start.5 = ((f32[2,1,128,8]{3,0,1,2:T(2,128)}), f32[2,1,128,8]{3,0,1,2:T(2,128)S(1)}, u32[]{:S(2)}, u32[]{:S(2)}) async-start(f32[2,1,128,8]{3,0,1,2:T(2,128)} %copy.989), calls=%async_computation.5 | async-start | bytes 262144 | tf_op jit(solution)/shard_map/all_to_all | solution.py:131
  210.7 3.0 collective-permute-start.14
  213.7 3.8 %all-to-all-done.5 = f32[2,1,128,8]{3,0,1,2:T(2,128)S(1)} async-done(((f32[2,1,128,8]{3,0,1,2:T(2,128)}), f32[2,1,128,8]{3,0,1,2:T(2,128)S(1)}, u32[]{:S(2)}, u32[]{:S(2)}) %all-to-all-start.5) | async-done | bytes 8224 | tf_op jit(solution)/shard_map/all_to_all | solution.py:131
  219.9 3.0 collective-permute-start.16
  223.4 3.4 collective-permute-start.26
  226.8 1.3 collective-permute-start.27
  228.6 1.4 collective-permute-done.27
  232.2 11.9 %all-to-all-start.4 = ((f32[2,1,4,256]{2,0,1,3:T(2,128)}), f32[2,1,4,256]{2,0,1,3:T(2,128)S(1)}, u32[]{:S(2)}, u32[]{:S(2)}) async-start(f32[2,1,4,256]{2,0,1,3:T(2,128)} %copy.981), calls=%async_computation.4 | async-start | bytes 524288 | tf_op jit(solution)/shard_map/all_to_all | solution.py:159
  244.5 40.5 %psum.30 = f32[1,128]{1,0:T(1,128)S(1)} all-reduce(f32[1,128]{1,0:T(1,128)S(1)} %fusion.3), channel_id=1, replica_groups=mesh['groups'=1,'gx'=32] {'gx'}, use_global_device_ids=true, to_apply=%region_10.11 | all-reduce | flops 128 | bytes 1024 | tf_op jit(solution)/shard_map/psum | solution.py:189
  286.8 1.3 collective-permute-start.28
  288.1 3.0 collective-permute-start.29
  292.6 6.2 %all-to-all-start.6 = ((f32[2,1,128,8]{3,0,1,2:T(2,128)}), f32[2,1,128,8]{3,0,1,2:T(2,128)S(1)}, u32[]{:S(2)}, u32[]{:S(2)}) async-start(f32[2,1,128,8]{3,0,1,2:T(2,128)} %copy.992), calls=%async_computation.6 | async-start | bytes 262144 | tf_op jit(solution)/shard_map/all_to_all | solution.py:131
  298.9 1.3 collective-permute-start.23
  300.2 3.0 collective-permute-start.22
  303.2 3.8 %all-to-all-done.6 = f32[2,1,128,8]{3,0,1,2:T(2,128)S(1)} async-done(((f32[2,1,128,8]{3,0,1,2:T(2,128)}), f32[2,1,128,8]{3,0,1,2:T(2,128)S(1)}, u32[]{:S(2)}, u32[]{:S(2)}) %all-to-all-start.6) | async-done | bytes 8224 | tf_op jit(solution)/shard_map/all_to_all | solution.py:131
  309.1 2.1 collective-permute-start.30
  311.2 1.3 collective-permute-start.31
  313.2 1.9 collective-permute-done.31
  316.8 46.5 %psum.31 = f32[1,128]{1,0:T(1,128)S(1)} all-reduce(f32[1,128]{1,0:T(1,128)S(1)} %fusion.1), channel_id=1, replica_groups=mesh['groups'=1,'gx'=32] {'gx'}, use_global_device_ids=true, to_apply=%region_13.14 | all-reduce | flops 128 | bytes 1024 | tf_op jit(solution)/shard_map/psum | solution.py:189
  365.1 1.4 fusion.372
  (226 shorter events, 40.5 us)
Async XLA Ops:
  0.6 6.1 %copy-start = (f32[9,2,1,8,4,128]{5,4,3,2,1,0:T(4,128)S(1)}, f32[9,2,1,8,4,128]{5,4,3,2,1,0:T(4,128)}, u32[]{:S(2)}) copy-start(f32[9,2,1,8,4,128]{5,4,3,2,1,0:T(4,128)} %param.34) | copy-start | bytes 884740
  1.6 41.8 %collective-permute-start.10 = (f32[2,1,4,12,256]{4,2,3,1,0:T(4,128)S(1)}, f32[2,1,4,12,256]{4,2,3,1,0:T(4,128)S(1)}, u32[]{:S(2)}, u32[]{:S(2)}) collective-permute-start(f32[2,1,4,12,256]{4,2,3,1,0:T(4,128)S(1)} %slice_bitcast_fusion.3), channel_id=1, source_target_pairs={{1,0},{2,1},{3,2},{4,3},{5,4},{6,5},{7,6},{8,7},{9,8},{10,9},{11,1... | collective-permute-start | bytes 294920 | tf_op jit(solution)/shard_map/ppermute | solution.py:18
  2.9 40.5 %collective-permute-start.11 = (f32[2,1,4,12,256]{4,2,3,1,0:T(4,128)S(1)}, f32[2,1,4,12,256]{4,2,3,1,0:T(4,128)S(1)}, u32[]{:S(2)}, u32[]{:S(2)}) collective-permute-start(f32[2,1,4,12,256]{4,2,3,1,0:T(4,128)S(1)} %slice_bitcast_fusion.3), channel_id=1, source_target_pairs={{0,1},{1,2},{2,3},{3,4},{4,5},{5,6},{6,7},{7,8},{8,9},{9,10},{10,1... | collective-permute-start | bytes 294920 | tf_op jit(solution)/shard_map/ppermute | solution.py:17
  6.8 6.4 %copy-start.7 = (s32[4,256]{1,0:T(4,128)S(1)}, s32[4,256]{1,0:T(4,128)}, u32[]{:S(2)}) copy-start(s32[4,256]{1,0:T(4,128)} %param.41) | copy-start | bytes 12292
  6.8 11.5 %collective-permute-start.1 = (f32[3,2,1,4,4,128]{5,4,3,2,1,0:T(4,128)S(1)}, f32[3,2,1,4,4,128]{5,4,3,2,1,0:T(4,128)S(1)}, u32[]{:S(2)}, u32[]{:S(2)}) collective-permute-start(f32[3,2,1,4,4,128]{5,4,3,2,1,0:T(4,128)S(1)} %get-tuple-element.249), channel_id=1, source_target_pairs={{1,0},{2,1},{3,2},{4,3},{5,4},{6,5},{7,6},{8,7},{9,8},{10,9},{11,1... | collective-permute-start | bytes 147464 | tf_op jit(solution)/shard_map/ppermute | solution.py:18
  8.1 10.3 %collective-permute-start = (f32[3,2,1,4,4,128]{5,4,3,2,1,0:T(4,128)S(1)}, f32[3,2,1,4,4,128]{5,4,3,2,1,0:T(4,128)S(1)}, u32[]{:S(2)}, u32[]{:S(2)}) collective-permute-start(f32[3,2,1,4,4,128]{5,4,3,2,1,0:T(4,128)S(1)} %get-tuple-element.248), channel_id=1, source_target_pairs={{0,1},{1,2},{2,3},{3,4},{4,5},{5,6},{6,7},{7,8},{8,9},{9,10},{10,1... | collective-permute-start | bytes 147464 | tf_op jit(solution)/shard_map/ppermute | solution.py:17
  13.3 0.7 copy-start.6
  14.0 0.7 copy-start.5
  14.7 0.8 copy-start.3
  15.5 0.8 copy-start.4
  19.5 18.0 %all-to-all-start.1 = ((f32[2,1,128,8]{3,0,1,2:T(2,128)}), f32[2,1,128,8]{3,0,1,2:T(2,128)S(1)}, u32[]{:S(2)}, u32[]{:S(2)}) async-start(f32[2,1,128,8]{3,0,1,2:T(2,128)} %copy.963), calls=%async_computation.1 | async-start | bytes 262144 | tf_op jit(solution)/shard_map/all_to_all | solution.py:131
  29.7 8.0 %copy-start.1 = (f32[4,2,1,4,12,256]{5,3,4,2,1,0:T(4,128)S(1)}, f32[4,2,1,4,12,256]{5,3,4,2,1,0:T(4,128)}, u32[]{:S(2)}) copy-start(f32[4,2,1,4,12,256]{5,3,4,2,1,0:T(4,128)} %param.35) | copy-start | bytes 1179652
  29.7 8.0 %collective-permute-start.3 = (f32[3,2,1,4,4,128]{5,4,3,2,1,0:T(4,128)S(1)}, f32[3,2,1,4,4,128]{5,4,3,2,1,0:T(4,128)S(1)}, u32[]{:S(2)}, u32[]{:S(2)}) collective-permute-start(f32[3,2,1,4,4,128]{5,4,3,2,1,0:T(4,128)S(1)} %get-tuple-element.247), channel_id=1, source_target_pairs={{1,0},{2,1},{3,2},{4,3},{5,4},{6,5},{7,6},{8,7},{9,8},{10,9},{11,1... | collective-permute-start | bytes 147464 | tf_op jit(solution)/shard_map/ppermute | solution.py:18
  31.2 6.6 %collective-permute-start.2 = (f32[3,2,1,4,4,128]{5,4,3,2,1,0:T(4,128)S(1)}, f32[3,2,1,4,4,128]{5,4,3,2,1,0:T(4,128)S(1)}, u32[]{:S(2)}, u32[]{:S(2)}) collective-permute-start(f32[3,2,1,4,4,128]{5,4,3,2,1,0:T(4,128)S(1)} %get-tuple-element.246), channel_id=1, source_target_pairs={{0,1},{1,2},{2,3},{3,4},{4,5},{5,6},{6,7},{7,8},{8,9},{9,10},{10,1... | collective-permute-start | bytes 147464 | tf_op jit(solution)/shard_map/ppermute | solution.py:17
  37.9 0.7 copy-start.2
  39.1 9.5 %collective-permute-start.5 = (f32[3,2,1,4,4,128]{5,4,3,2,1,0:T(4,128)S(1)}, f32[3,2,1,4,4,128]{5,4,3,2,1,0:T(4,128)S(1)}, u32[]{:S(2)}, u32[]{:S(2)}) collective-permute-start(f32[3,2,1,4,4,128]{5,4,3,2,1,0:T(4,128)S(1)} %get-tuple-element.245), channel_id=1, source_target_pairs={{1,0},{2,1},{3,2},{4,3},{5,4},{6,5},{7,6},{8,7},{9,8},{10,9},{11,1... | collective-permute-start | bytes 147464 | tf_op jit(solution)/shard_map/ppermute | solution.py:18
  40.4 8.2 %collective-permute-start.4 = (f32[3,2,1,4,4,128]{5,4,3,2,1,0:T(4,128)S(1)}, f32[3,2,1,4,4,128]{5,4,3,2,1,0:T(4,128)S(1)}, u32[]{:S(2)}, u32[]{:S(2)}) collective-permute-start(f32[3,2,1,4,4,128]{5,4,3,2,1,0:T(4,128)S(1)} %get-tuple-element.244), channel_id=1, source_target_pairs={{0,1},{1,2},{2,3},{3,4},{4,5},{5,6},{6,7},{7,8},{8,9},{9,10},{10,1... | collective-permute-start | bytes 147464 | tf_op jit(solution)/shard_map/ppermute | solution.py:17
  43.9 5.2 %collective-permute-start.12 = (f32[2,1,4,12,256]{4,2,3,1,0:T(4,128)S(1)}, f32[2,1,4,12,256]{4,2,3,1,0:T(4,128)S(1)}, u32[]{:S(2)}, u32[]{:S(2)}) collective-permute-start(f32[2,1,4,12,256]{4,2,3,1,0:T(4,128)S(1)} %get-tuple-element.190), channel_id=1, source_target_pairs={{0,1},{1,2},{2,3},{3,4},{4,5},{5,6},{6,7},{7,8},{8,9},{9,10},{10,1... | collective-permute-start | bytes 294920 | tf_op jit(solution)/shard_map/ppermute | solution.py:17
  47.3 3.2 collective-permute-start.13
  52.6 59.5 %all-to-all-start = ((f32[2,1,4,256]{2,0,1,3:T(2,128)}), f32[2,1,4,256]{2,0,1,3:T(2,128)S(1)}, u32[]{:S(2)}, u32[]{:S(2)}) async-start(f32[2,1,4,256]{2,0,1,3:T(2,128)} %copy.948), calls=%async_computation | async-start | bytes 524288 | tf_op jit(solution)/shard_map/all_to_all | solution.py:159
  65.1 40.9 %copy-start.10 = (f32[4,1,128]{2,1,0:T(1,128)S(1)}, f32[4,1,128]{2,1,0:T(1,128)}, u32[]{:S(2)}) copy-start(f32[4,1,128]{2,1,0:T(1,128)} %param.45) | copy-start | bytes 6148
  107.8 25.7 %collective-permute-start.18 = (f32[2,1,4,12,256]{4,2,3,1,0:T(4,128)S(1)}, f32[2,1,4,12,256]{4,2,3,1,0:T(4,128)S(1)}, u32[]{:S(2)}, u32[]{:S(2)}) collective-permute-start(f32[2,1,4,12,256]{4,2,3,1,0:T(4,128)S(1)} %fusion.1104), channel_id=1, source_target_pairs={{1,0},{2,1},{3,2},{4,3},{5,4},{6,5},{7,6},{8,7},{9,8},{10,9},{11,1... | collective-permute-start | bytes 294920 | tf_op jit(solution)/shard_map/ppermute | solution.py:18
  109.1 24.4 %collective-permute-start.19 = (f32[2,1,4,12,256]{4,2,3,1,0:T(4,128)S(1)}, f32[2,1,4,12,256]{4,2,3,1,0:T(4,128)S(1)}, u32[]{:S(2)}, u32[]{:S(2)}) collective-permute-start(f32[2,1,4,12,256]{4,2,3,1,0:T(4,128)S(1)} %fusion.1104), channel_id=1, source_target_pairs={{0,1},{1,2},{2,3},{3,4},{4,5},{5,6},{6,7},{7,8},{8,9},{9,10},{10,1... | collective-permute-start | bytes 294920 | tf_op jit(solution)/shard_map/ppermute | solution.py:17
  113.6 14.4 %all-to-all-start.3 = ((f32[2,1,128,8]{3,0,1,2:T(2,128)}), f32[2,1,128,8]{3,0,1,2:T(2,128)S(1)}, u32[]{:S(2)}, u32[]{:S(2)}) async-start(f32[2,1,128,8]{3,0,1,2:T(2,128)} %copy.978), calls=%async_computation.3 | async-start | bytes 262144 | tf_op jit(solution)/shard_map/all_to_all | solution.py:131
  119.9 8.4 %collective-permute-start.7 = (f32[3,2,1,4,4,128]{5,4,3,2,1,0:T(4,128)S(1)}, f32[3,2,1,4,4,128]{5,4,3,2,1,0:T(4,128)S(1)}, u32[]{:S(2)}, u32[]{:S(2)}) collective-permute-start(f32[3,2,1,4,4,128]{5,4,3,2,1,0:T(4,128)S(1)} %get-tuple-element.243), channel_id=1, source_target_pairs={{1,0},{2,1},{3,2},{4,3},{5,4},{6,5},{7,6},{8,7},{9,8},{10,9},{11,1... | collective-permute-start | bytes 147464 | tf_op jit(solution)/shard_map/ppermute | solution.py:18
  121.2 7.2 %collective-permute-start.6 = (f32[3,2,1,4,4,128]{5,4,3,2,1,0:T(4,128)S(1)}, f32[3,2,1,4,4,128]{5,4,3,2,1,0:T(4,128)S(1)}, u32[]{:S(2)}, u32[]{:S(2)}) collective-permute-start(f32[3,2,1,4,4,128]{5,4,3,2,1,0:T(4,128)S(1)} %get-tuple-element.242), channel_id=1, source_target_pairs={{0,1},{1,2},{2,3},{3,4},{4,5},{5,6},{6,7},{7,8},{8,9},{9,10},{10,1... | collective-permute-start | bytes 147464 | tf_op jit(solution)/shard_map/ppermute | solution.py:17
  129.1 9.5 %collective-permute-start.9 = (f32[3,2,1,4,4,128]{5,4,3,2,1,0:T(4,128)S(1)}, f32[3,2,1,4,4,128]{5,4,3,2,1,0:T(4,128)S(1)}, u32[]{:S(2)}, u32[]{:S(2)}) collective-permute-start(f32[3,2,1,4,4,128]{5,4,3,2,1,0:T(4,128)S(1)} %get-tuple-element.241), channel_id=1, source_target_pairs={{1,0},{2,1},{3,2},{4,3},{5,4},{6,5},{7,6},{8,7},{9,8},{10,9},{11,1... | collective-permute-start | bytes 147464 | tf_op jit(solution)/shard_map/ppermute | solution.py:18
  130.4 8.2 %collective-permute-start.8 = (f32[3,2,1,4,4,128]{5,4,3,2,1,0:T(4,128)S(1)}, f32[3,2,1,4,4,128]{5,4,3,2,1,0:T(4,128)S(1)}, u32[]{:S(2)}, u32[]{:S(2)}) collective-permute-start(f32[3,2,1,4,4,128]{5,4,3,2,1,0:T(4,128)S(1)} %get-tuple-element.240), channel_id=1, source_target_pairs={{0,1},{1,2},{2,3},{3,4},{4,5},{5,6},{6,7},{7,8},{8,9},{9,10},{10,1... | collective-permute-start | bytes 147464 | tf_op jit(solution)/shard_map/ppermute | solution.py:17
  133.9 5.2 %collective-permute-start.20 = (f32[2,1,4,12,256]{4,2,3,1,0:T(4,128)S(1)}, f32[2,1,4,12,256]{4,2,3,1,0:T(4,128)S(1)}, u32[]{:S(2)}, u32[]{:S(2)}) collective-permute-start(f32[2,1,4,12,256]{4,2,3,1,0:T(4,128)S(1)} %get-tuple-element.220), channel_id=1, source_target_pairs={{0,1},{1,2},{2,3},{3,4},{4,5},{5,6},{6,7},{7,8},{8,9},{9,10},{10,1... | collective-permute-start | bytes 294920 | tf_op jit(solution)/shard_map/ppermute | solution.py:17
  137.3 3.2 collective-permute-start.21
  142.7 59.0 %all-to-all-start.2 = ((f32[2,1,4,256]{2,0,1,3:T(2,128)}), f32[2,1,4,256]{2,0,1,3:T(2,128)S(1)}, u32[]{:S(2)}, u32[]{:S(2)}) async-start(f32[2,1,4,256]{2,0,1,3:T(2,128)} %copy.966), calls=%async_computation.2 | async-start | bytes 524288 | tf_op jit(solution)/shard_map/all_to_all | solution.py:159
  197.3 25.7 %collective-permute-start.24 = (f32[2,1,4,12,256]{4,2,3,1,0:T(4,128)S(1)}, f32[2,1,4,12,256]{4,2,3,1,0:T(4,128)S(1)}, u32[]{:S(2)}, u32[]{:S(2)}) collective-permute-start(f32[2,1,4,12,256]{4,2,3,1,0:T(4,128)S(1)} %fusion.1105), channel_id=1, source_target_pairs={{1,0},{2,1},{3,2},{4,3},{5,4},{6,5},{7,6},{8,7},{9,8},{10,9},{11,1... | collective-permute-start | bytes 294920 | tf_op jit(solution)/shard_map/ppermute | solution.py:18
  198.6 24.4 %collective-permute-start.25 = (f32[2,1,4,12,256]{4,2,3,1,0:T(4,128)S(1)}, f32[2,1,4,12,256]{4,2,3,1,0:T(4,128)S(1)}, u32[]{:S(2)}, u32[]{:S(2)}) collective-permute-start(f32[2,1,4,12,256]{4,2,3,1,0:T(4,128)S(1)} %fusion.1105), channel_id=1, source_target_pairs={{0,1},{1,2},{2,3},{3,4},{4,5},{5,6},{6,7},{7,8},{8,9},{9,10},{10,1... | collective-permute-start | bytes 294920 | tf_op jit(solution)/shard_map/ppermute | solution.py:17
  203.1 14.4 %all-to-all-start.5 = ((f32[2,1,128,8]{3,0,1,2:T(2,128)}), f32[2,1,128,8]{3,0,1,2:T(2,128)S(1)}, u32[]{:S(2)}, u32[]{:S(2)}) async-start(f32[2,1,128,8]{3,0,1,2:T(2,128)} %copy.989), calls=%async_computation.5 | async-start | bytes 262144 | tf_op jit(solution)/shard_map/all_to_all | solution.py:131
  209.4 8.4 %collective-permute-start.15 = (f32[3,2,1,4,4,128]{5,4,3,2,1,0:T(4,128)S(1)}, f32[3,2,1,4,4,128]{5,4,3,2,1,0:T(4,128)S(1)}, u32[]{:S(2)}, u32[]{:S(2)}) collective-permute-start(f32[3,2,1,4,4,128]{5,4,3,2,1,0:T(4,128)S(1)} %get-tuple-element.239), channel_id=1, source_target_pairs={{1,0},{2,1},{3,2},{4,3},{5,4},{6,5},{7,6},{8,7},{9,8},{10,9},{11,1... | collective-permute-start | bytes 147464 | tf_op jit(solution)/shard_map/ppermute | solution.py:18
  210.7 7.2 %collective-permute-start.14 = (f32[3,2,1,4,4,128]{5,4,3,2,1,0:T(4,128)S(1)}, f32[3,2,1,4,4,128]{5,4,3,2,1,0:T(4,128)S(1)}, u32[]{:S(2)}, u32[]{:S(2)}) collective-permute-start(f32[3,2,1,4,4,128]{5,4,3,2,1,0:T(4,128)S(1)} %get-tuple-element.238), channel_id=1, source_target_pairs={{0,1},{1,2},{2,3},{3,4},{4,5},{5,6},{6,7},{7,8},{8,9},{9,10},{10,1... | collective-permute-start | bytes 147464 | tf_op jit(solution)/shard_map/ppermute | solution.py:17
  218.6 9.5 %collective-permute-start.17 = (f32[3,2,1,4,4,128]{5,4,3,2,1,0:T(4,128)S(1)}, f32[3,2,1,4,4,128]{5,4,3,2,1,0:T(4,128)S(1)}, u32[]{:S(2)}, u32[]{:S(2)}) collective-permute-start(f32[3,2,1,4,4,128]{5,4,3,2,1,0:T(4,128)S(1)} %get-tuple-element.237), channel_id=1, source_target_pairs={{1,0},{2,1},{3,2},{4,3},{5,4},{6,5},{7,6},{8,7},{9,8},{10,9},{11,1... | collective-permute-start | bytes 147464 | tf_op jit(solution)/shard_map/ppermute | solution.py:18
  219.9 8.2 %collective-permute-start.16 = (f32[3,2,1,4,4,128]{5,4,3,2,1,0:T(4,128)S(1)}, f32[3,2,1,4,4,128]{5,4,3,2,1,0:T(4,128)S(1)}, u32[]{:S(2)}, u32[]{:S(2)}) collective-permute-start(f32[3,2,1,4,4,128]{5,4,3,2,1,0:T(4,128)S(1)} %get-tuple-element.236), channel_id=1, source_target_pairs={{0,1},{1,2},{2,3},{3,4},{4,5},{5,6},{6,7},{7,8},{8,9},{9,10},{10,1... | collective-permute-start | bytes 147464 | tf_op jit(solution)/shard_map/ppermute | solution.py:17
  223.4 5.2 %collective-permute-start.26 = (f32[2,1,4,12,256]{4,2,3,1,0:T(4,128)S(1)}, f32[2,1,4,12,256]{4,2,3,1,0:T(4,128)S(1)}, u32[]{:S(2)}, u32[]{:S(2)}) collective-permute-start(f32[2,1,4,12,256]{4,2,3,1,0:T(4,128)S(1)} %get-tuple-element.212), channel_id=1, source_target_pairs={{0,1},{1,2},{2,3},{3,4},{4,5},{5,6},{6,7},{7,8},{8,9},{9,10},{10,1... | collective-permute-start | bytes 294920 | tf_op jit(solution)/shard_map/ppermute | solution.py:17
  226.8 3.2 collective-permute-start.27
  232.2 59.0 %all-to-all-start.4 = ((f32[2,1,4,256]{2,0,1,3:T(2,128)}), f32[2,1,4,256]{2,0,1,3:T(2,128)S(1)}, u32[]{:S(2)}, u32[]{:S(2)}) async-start(f32[2,1,4,256]{2,0,1,3:T(2,128)} %copy.981), calls=%async_computation.4 | async-start | bytes 524288 | tf_op jit(solution)/shard_map/all_to_all | solution.py:159
  286.8 21.9 %collective-permute-start.28 = (f32[2,1,4,12,256]{4,2,3,1,0:T(4,128)S(1)}, f32[2,1,4,12,256]{4,2,3,1,0:T(4,128)S(1)}, u32[]{:S(2)}, u32[]{:S(2)}) collective-permute-start(f32[2,1,4,12,256]{4,2,3,1,0:T(4,128)S(1)} %fusion.1106), channel_id=1, source_target_pairs={{1,0},{2,1},{3,2},{4,3},{5,4},{6,5},{7,6},{8,7},{9,8},{10,9},{11,1... | collective-permute-start | bytes 294920 | tf_op jit(solution)/shard_map/ppermute | solution.py:18
  288.1 20.6 %collective-permute-start.29 = (f32[2,1,4,12,256]{4,2,3,1,0:T(4,128)S(1)}, f32[2,1,4,12,256]{4,2,3,1,0:T(4,128)S(1)}, u32[]{:S(2)}, u32[]{:S(2)}) collective-permute-start(f32[2,1,4,12,256]{4,2,3,1,0:T(4,128)S(1)} %fusion.1106), channel_id=1, source_target_pairs={{0,1},{1,2},{2,3},{3,4},{4,5},{5,6},{6,7},{7,8},{8,9},{9,10},{10,1... | collective-permute-start | bytes 294920 | tf_op jit(solution)/shard_map/ppermute | solution.py:17
  292.6 14.4 %all-to-all-start.6 = ((f32[2,1,128,8]{3,0,1,2:T(2,128)}), f32[2,1,128,8]{3,0,1,2:T(2,128)S(1)}, u32[]{:S(2)}, u32[]{:S(2)}) async-start(f32[2,1,128,8]{3,0,1,2:T(2,128)} %copy.992), calls=%async_computation.6 | async-start | bytes 262144 | tf_op jit(solution)/shard_map/all_to_all | solution.py:131
  298.9 8.4 %collective-permute-start.23 = (f32[3,2,1,4,4,128]{5,4,3,2,1,0:T(4,128)S(1)}, f32[3,2,1,4,4,128]{5,4,3,2,1,0:T(4,128)S(1)}, u32[]{:S(2)}, u32[]{:S(2)}) collective-permute-start(f32[3,2,1,4,4,128]{5,4,3,2,1,0:T(4,128)S(1)} %get-tuple-element.235), channel_id=1, source_target_pairs={{1,0},{2,1},{3,2},{4,3},{5,4},{6,5},{7,6},{8,7},{9,8},{10,9},{11,1... | collective-permute-start | bytes 147464 | tf_op jit(solution)/shard_map/ppermute | solution.py:18
  300.2 7.2 %collective-permute-start.22 = (f32[3,2,1,4,4,128]{5,4,3,2,1,0:T(4,128)S(1)}, f32[3,2,1,4,4,128]{5,4,3,2,1,0:T(4,128)S(1)}, u32[]{:S(2)}, u32[]{:S(2)}) collective-permute-start(f32[3,2,1,4,4,128]{5,4,3,2,1,0:T(4,128)S(1)} %get-tuple-element.234), channel_id=1, source_target_pairs={{0,1},{1,2},{2,3},{3,4},{4,5},{5,6},{6,7},{7,8},{8,9},{9,10},{10,1... | collective-permute-start | bytes 147464 | tf_op jit(solution)/shard_map/ppermute | solution.py:17
  309.1 4.1 %collective-permute-start.30 = (f32[2,1,4,12,256]{4,2,3,1,0:T(4,128)S(1)}, f32[2,1,4,12,256]{4,2,3,1,0:T(4,128)S(1)}, u32[]{:S(2)}, u32[]{:S(2)}) collective-permute-start(f32[2,1,4,12,256]{4,2,3,1,0:T(4,128)S(1)} %get-tuple-element.204), channel_id=1, source_target_pairs={{0,1},{1,2},{2,3},{3,4},{4,5},{5,6},{6,7},{7,8},{8,9},{9,10},{10,1... | collective-permute-start | bytes 294920 | tf_op jit(solution)/shard_map/ppermute | solution.py:17
  311.2 3.9 %collective-permute-start.31 = (f32[2,1,4,12,256]{4,2,3,1,0:T(4,128)S(1)}, f32[2,1,4,12,256]{4,2,3,1,0:T(4,128)S(1)}, u32[]{:S(2)}, u32[]{:S(2)}) collective-permute-start(f32[2,1,4,12,256]{4,2,3,1,0:T(4,128)S(1)} %get-tuple-element.204), channel_id=1, source_target_pairs={{1,0},{2,1},{3,2},{4,3},{5,4},{6,5},{7,6},{8,7},{9,8},{10,9},{11,1... | collective-permute-start | bytes 294920 | tf_op jit(solution)/shard_map/ppermute | solution.py:18
  (2 other events, 1.3 us)
where the time goes:
time: 369 us; the launch traced here: 367 us
  blocking collectives  168 us (46%)
  starting transfers between devices  136 us (37%)
  waiting for transfers between devices  21 us (6%)
  other arithmetic  18.8 us (5%)
  local copies, waits for them, and re-layouts  14.5 us (4%)
  between operations  5.44 us (1%)
    psum x4, blocking collectives, on_device(): recorded = lax.psum(partial_record, 'gx')  168 us
    ppermute x16, starting transfers between devices, with_halo(): before = lax.ppermute(last, axis, up)  50.7 us
    all_to_all x3, starting transfers between devices, on_device(): lax.all_to_all(floor_pressure, 'gx', split_axis=3, concat_axis=2, tiled=T...  36.3 us
    all_to_all x4, starting transfers between devices, on_device(): lax.all_to_all(jnp.transpose(vel_z[:, :, :, 0, :], (0, 1, 3, 2)), 'gx', s...  28.3 us
    ppermute x16, starting transfers between devices, with_halo(): after = lax.ppermute(first, axis, down)  20.8 us
    all_to_all x4, waiting for transfers between devices, on_device(): lax.all_to_all(jnp.transpose(vel_z[:, :, :, 0, :], (0, 1, 3, 2)), 'gx', s...  14.8 us
  transfers between devices with their start and end apart: 39, of which 8 were waited for; matrix products, arithmetic and copies ran while one was open for 5% of the time, Pallas kernels for 0%

commit v1 on v0

--- a/solution.py
+++ b/solution.py
@@ -186,7 +186,7 @@
             node_hot,
             precision=lax.Precision.HIGHEST,
         )
-        recorded = lax.psum(partial_record, "gx")
+        recorded = jnp.sum(lax.all_gather(partial_record, "gx"), axis=0)
         misfit = recorded - observed[step]
         scaled = misfit * lax.rsqrt(jnp.mean(misfit * misfit, axis=1, keepdims=True) + 1e-06)
         inject = jnp.dot(

time: 369 us -> 351 us (0.951)
  starting transfers between devices: 136 us -> 96.9 us
  waiting for transfers between devices: 21 us -> 36 us
  blocking collectives: 168 us -> 174 us
    all_gather x0 -> x4, blocking collectives: none -> 174 us  [on_device(): recorded = jnp.sum(lax.all_gather(partial_record, 'gx'), axis=0)]
    psum x4 -> x0, blocking collectives: 168 us -> none  [on_device(): recorded = lax.psum(partial_record, 'gx')]
    all_to_all x3, starting transfers between devices: 36.3 us -> 7.75 us  [on_device(): lax.all_to_all(floor_pressure, 'gx', split_axis=3, concat_axis=2, tiled=T...]
    all_to_all x3, waiting for transfers between devices: 0.01 us -> 15.2 us  [on_device(): lax.all_to_all(floor_pressure, 'gx', split_axis=3, concat_axis=2, tiled=T...]
    all_to_all x4, starting transfers between devices: 28.3 us -> 17.5 us  [on_device(): lax.all_to_all(jnp.transpose(vel_z[:, :, :, 0, :], (0, 1, 3, 2)), 'gx', s...]
  transfers between devices with their start and end apart: 39 -> 39, of which waited for: 8 -> 11; matrix products, arithmetic and copies ran while one was open for 5% -> 5% of each run, Pallas kernels for 0% -> 0%
where the time goes in v1:
time: 351 us; the launch traced here: 349 us
  blocking collectives  174 us (50%)
  starting transfers between devices  96.9 us (28%)
  waiting for transfers between devices  36 us (10%)
  other arithmetic  19 us (5%)
  local copies, waits for them, and re-layouts  15.1 us (4%)
  between operations  5.4 us (2%)
    all_gather x4, blocking collectives, on_device(): recorded = jnp.sum(lax.all_gather(partial_record, 'gx'), axis=0)  174 us
    ppermute x16, starting transfers between devices, with_halo(): before = lax.ppermute(last, axis, up)  50.9 us
    ppermute x16, starting transfers between devices, with_halo(): after = lax.ppermute(first, axis, down)  20.8 us
    all_to_all x4, starting transfers between devices, on_device(): lax.all_to_all(jnp.transpose(vel_z[:, :, :, 0, :], (0, 1, 3, 2)), 'gx', s...  17.5 us
    all_to_all x3, waiting for transfers between devices, on_device(): lax.all_to_all(floor_pressure, 'gx', split_axis=3, concat_axis=2, tiled=T...  15.2 us
    all_to_all x4, waiting for transfers between devices, on_device(): lax.all_to_all(jnp.transpose(vel_z[:, :, :, 0, :], (0, 1, 3, 2)), 'gx', s...  14.6 us
    all_to_all x3, starting transfers between devices, on_device(): lax.all_to_all(floor_pressure, 'gx', split_axis=3, concat_axis=2, tiled=T...  7.75 us
  transfers between devices with their start and end apart: 39, of which 11 were waited for; matrix products, arithmetic and copies ran while one was open for 5% of the time, Pallas kernels for 0%

profile of v1, /device:TPU:0, one launch (start us, length us, event | category | flops | bytes accessed | tf_op | source)
XLA Modules:
  0.0 349.3 jit_solution(11933936070988885286)
XLA Ops:
  2.9 3.0 collective-permute-start.11
  6.8 1.3 collective-permute-start.1
  8.1 5.1 %collective-permute-start = (f32[3,2,1,4,4,128]{5,4,3,2,1,0:T(4,128)S(1)}, f32[3,2,1,4,4,128]{5,4,3,2,1,0:T(4,128)S(1)}, u32[]{:S(2)}, u32[]{:S(2)}) collective-permute-start(f32[3,2,1,4,4,128]{5,4,3,2,1,0:T(4,128)S(1)} %get-tuple-element.248), channel_id=1, source_target_pairs={{0,1},{1,2},{2,3},{3,4},{4,5},{5,6},{6,7},{7,8},{8,9},{9,10},{10,1... | collective-permute-start | bytes 147464 | tf_op jit(solution)/shard_map/ppermute | solution.py:17
  19.5 9.7 %all-to-all-start.1 = ((f32[2,1,128,8]{3,0,1,2:T(2,128)}), f32[2,1,128,8]{3,0,1,2:T(2,128)S(1)}, u32[]{:S(2)}, u32[]{:S(2)}) async-start(f32[2,1,128,8]{3,0,1,2:T(2,128)} %copy.963), calls=%async_computation.1 | async-start | bytes 262144 | tf_op jit(solution)/shard_map/all_to_all | solution.py:131
  29.7 1.4 collective-permute-start.3
  31.2 3.0 collective-permute-start.2
  34.2 3.3 all-to-all-done.1
  39.1 1.3 collective-permute-start.5
  40.4 3.0 collective-permute-start.4
  43.9 3.4 collective-permute-start.12
  47.3 1.3 collective-permute-start.13
  49.1 1.4 collective-permute-done.13
  52.2 43.7 %all-gather.4 = f32[32,1,128]{2,1,0:T(1,128)S(1)} all-gather(f32[1,1,128]{2,1,0:T(1,128)S(1)} %convolution_bitcast_fusion.3), channel_id=2, replica_groups=mesh['groups'=1,'gx'=32] {'gx'}, dimensions={0}, use_global_device_ids=true | all-gather | bytes 16896 | tf_op jit(solution)/shard_map/all_gather | solution.py:189
  98.0 2.6 all-to-all-start
  101.8 1.3 collective-permute-start.18
  103.1 3.0 collective-permute-start.19
  106.2 5.1 %all-to-all-done = f32[2,1,4,256]{2,0,1,3:T(2,128)S(1)} async-done(((f32[2,1,4,256]{2,0,1,3:T(2,128)}), f32[2,1,4,256]{2,0,1,3:T(2,128)S(1)}, u32[]{:S(2)}, u32[]{:S(2)}) %all-to-all-start) | async-done | bytes 8224 | tf_op jit(solution)/shard_map/all_to_all | solution.py:159
  112.7 2.6 all-to-all-start.3
  115.4 1.3 collective-permute-start.7
  116.7 3.0 collective-permute-start.6
  119.7 3.8 %all-to-all-done.3 = f32[2,1,128,8]{3,0,1,2:T(2,128)S(1)} async-done(((f32[2,1,128,8]{3,0,1,2:T(2,128)}), f32[2,1,128,8]{3,0,1,2:T(2,128)S(1)}, u32[]{:S(2)}, u32[]{:S(2)}) %all-to-all-start.3) | async-done | bytes 8224 | tf_op jit(solution)/shard_map/all_to_all | solution.py:131
  125.9 3.0 collective-permute-start.8
  129.4 3.4 collective-permute-start.20
  132.8 1.3 collective-permute-start.21
  134.6 1.4 collective-permute-done.21
  137.7 43.2 %all-gather.5 = f32[32,1,128]{2,1,0:T(1,128)S(1)} all-gather(f32[1,1,128]{2,1,0:T(1,128)S(1)} %convolution_bitcast_fusion.2), channel_id=3, replica_groups=mesh['groups'=1,'gx'=32] {'gx'}, dimensions={0}, use_global_device_ids=true | all-gather | bytes 16896 | tf_op jit(solution)/shard_map/all_gather | solution.py:189
  182.4 2.6 all-to-all-start.2
  186.2 1.3 collective-permute-start.24
  187.5 3.0 collective-permute-start.25
  190.5 5.1 %all-to-all-done.2 = f32[2,1,4,256]{2,0,1,3:T(2,128)S(1)} async-done(((f32[2,1,4,256]{2,0,1,3:T(2,128)}), f32[2,1,4,256]{2,0,1,3:T(2,128)S(1)}, u32[]{:S(2)}, u32[]{:S(2)}) %all-to-all-start.2) | async-done | bytes 8224 | tf_op jit(solution)/shard_map/all_to_all | solution.py:159
  197.1 2.6 all-to-all-start.5
  199.7 1.3 collective-permute-start.15
  201.0 3.2 collective-permute-start.14
  204.3 3.7 %all-to-all-done.5 = f32[2,1,128,8]{3,0,1,2:T(2,128)S(1)} async-done(((f32[2,1,128,8]{3,0,1,2:T(2,128)}), f32[2,1,128,8]{3,0,1,2:T(2,128)S(1)}, u32[]{:S(2)}, u32[]{:S(2)}) %all-to-all-start.5) | async-done | bytes 8224 | tf_op jit(solution)/shard_map/all_to_all | solution.py:131
  210.3 3.0 collective-permute-start.16
  213.8 3.4 collective-permute-start.26
  219.0 1.4 collective-permute-done.27
  222.1 43.2 %all-gather.6 = f32[32,1,128]{2,1,0:T(1,128)S(1)} all-gather(f32[1,1,128]{2,1,0:T(1,128)S(1)} %convolution_bitcast_fusion.1), channel_id=4, replica_groups=mesh['groups'=1,'gx'=32] {'gx'}, dimensions={0}, use_global_device_ids=true | all-gather | bytes 16896 | tf_op jit(solution)/shard_map/all_gather | solution.py:189
  266.8 2.6 all-to-all-start.4
  271.9 3.0 collective-permute-start.29
  274.9 5.1 %all-to-all-done.4 = f32[2,1,4,256]{2,0,1,3:T(2,128)S(1)} async-done(((f32[2,1,4,256]{2,0,1,3:T(2,128)}), f32[2,1,4,256]{2,0,1,3:T(2,128)S(1)}, u32[]{:S(2)}, u32[]{:S(2)}) %all-to-all-start.4) | async-done | bytes 8224 | tf_op jit(solution)/shard_map/all_to_all | solution.py:159
  281.5 2.6 all-to-all-start.6
  285.4 3.0 collective-permute-start.22
  288.5 3.8 %all-to-all-done.6 = f32[2,1,128,8]{3,0,1,2:T(2,128)S(1)} async-done(((f32[2,1,128,8]{3,0,1,2:T(2,128)}), f32[2,1,128,8]{3,0,1,2:T(2,128)S(1)}, u32[]{:S(2)}, u32[]{:S(2)}) %all-to-all-start.6) | async-done | bytes 8224 | tf_op jit(solution)/shard_map/all_to_all | solution.py:131
  294.4 2.1 collective-permute-start.30
  298.4 1.9 collective-permute-done.31
  302.1 43.5 %all-gather.7 = f32[32,1,128]{2,1,0:T(1,128)S(1)} all-gather(f32[1,1,128]{2,1,0:T(1,128)S(1)} %convolution_bitcast_fusion), channel_id=5, replica_groups=mesh['groups'=1,'gx'=32] {'gx'}, dimensions={0}, use_global_device_ids=true | all-gather | bytes 16896 | tf_op jit(solution)/shard_map/all_gather | solution.py:189
  348.0 1.4 fusion.368
  (234 shorter events, 45.2 us)
Async XLA Ops:
  0.6 6.1 %copy-start = (f32[9,2,1,8,4,128]{5,4,3,2,1,0:T(4,128)S(1)}, f32[9,2,1,8,4,128]{5,4,3,2,1,0:T(4,128)}, u32[]{:S(2)}) copy-start(f32[9,2,1,8,4,128]{5,4,3,2,1,0:T(4,128)} %param.34) | copy-start | bytes 884740
  1.6 41.8 %collective-permute-start.10 = (f32[2,1,4,12,256]{4,2,3,1,0:T(4,128)S(1)}, f32[2,1,4,12,256]{4,2,3,1,0:T(4,128)S(1)}, u32[]{:S(2)}, u32[]{:S(2)}) collective-permute-start(f32[2,1,4,12,256]{4,2,3,1,0:T(4,128)S(1)} %slice_bitcast_fusion.3), channel_id=1, source_target_pairs={{1,0},{2,1},{3,2},{4,3},{5,4},{6,5},{7,6},{8,7},{9,8},{10,9},{11,1... | collective-permute-start | bytes 294920 | tf_op jit(solution)/shard_map/ppermute | solution.py:18
  2.9 40.5 %collective-permute-start.11 = (f32[2,1,4,12,256]{4,2,3,1,0:T(4,128)S(1)}, f32[2,1,4,12,256]{4,2,3,1,0:T(4,128)S(1)}, u32[]{:S(2)}, u32[]{:S(2)}) collective-permute-start(f32[2,1,4,12,256]{4,2,3,1,0:T(4,128)S(1)} %slice_bitcast_fusion.3), channel_id=1, source_target_pairs={{0,1},{1,2},{2,3},{3,4},{4,5},{5,6},{6,7},{7,8},{8,9},{9,10},{10,1... | collective-permute-start | bytes 294920 | tf_op jit(solution)/shard_map/ppermute | solution.py:17
  6.8 6.4 %copy-start.7 = (s32[4,256]{1,0:T(4,128)S(1)}, s32[4,256]{1,0:T(4,128)}, u32[]{:S(2)}) copy-start(s32[4,256]{1,0:T(4,128)} %param.41) | copy-start | bytes 12292
  6.8 11.5 %collective-permute-start.1 = (f32[3,2,1,4,4,128]{5,4,3,2,1,0:T(4,128)S(1)}, f32[3,2,1,4,4,128]{5,4,3,2,1,0:T(4,128)S(1)}, u32[]{:S(2)}, u32[]{:S(2)}) collective-permute-start(f32[3,2,1,4,4,128]{5,4,3,2,1,0:T(4,128)S(1)} %get-tuple-element.249), channel_id=1, source_target_pairs={{1,0},{2,1},{3,2},{4,3},{5,4},{6,5},{7,6},{8,7},{9,8},{10,9},{11,1... | collective-permute-start | bytes 147464 | tf_op jit(solution)/shard_map/ppermute | solution.py:18
  8.1 10.3 %collective-permute-start = (f32[3,2,1,4,4,128]{5,4,3,2,1,0:T(4,128)S(1)}, f32[3,2,1,4,4,128]{5,4,3,2,1,0:T(4,128)S(1)}, u32[]{:S(2)}, u32[]{:S(2)}) collective-permute-start(f32[3,2,1,4,4,128]{5,4,3,2,1,0:T(4,128)S(1)} %get-tuple-element.248), channel_id=1, source_target_pairs={{0,1},{1,2},{2,3},{3,4},{4,5},{5,6},{6,7},{7,8},{8,9},{9,10},{10,1... | collective-permute-start | bytes 147464 | tf_op jit(solution)/shard_map/ppermute | solution.py:17
  13.3 0.7 copy-start.6
  14.0 0.7 copy-start.5
  14.7 0.8 copy-start.3
  15.5 0.8 copy-start.4
  19.5 18.0 %all-to-all-start.1 = ((f32[2,1,128,8]{3,0,1,2:T(2,128)}), f32[2,1,128,8]{3,0,1,2:T(2,128)S(1)}, u32[]{:S(2)}, u32[]{:S(2)}) async-start(f32[2,1,128,8]{3,0,1,2:T(2,128)} %copy.963), calls=%async_computation.1 | async-start | bytes 262144 | tf_op jit(solution)/shard_map/all_to_all | solution.py:131
  29.7 8.0 %copy-start.1 = (f32[4,2,1,4,12,256]{5,3,4,2,1,0:T(4,128)S(1)}, f32[4,2,1,4,12,256]{5,3,4,2,1,0:T(4,128)}, u32[]{:S(2)}) copy-start(f32[4,2,1,4,12,256]{5,3,4,2,1,0:T(4,128)} %param.35) | copy-start | bytes 1179652
  29.7 8.0 %collective-permute-start.3 = (f32[3,2,1,4,4,128]{5,4,3,2,1,0:T(4,128)S(1)}, f32[3,2,1,4,4,128]{5,4,3,2,1,0:T(4,128)S(1)}, u32[]{:S(2)}, u32[]{:S(2)}) collective-permute-start(f32[3,2,1,4,4,128]{5,4,3,2,1,0:T(4,128)S(1)} %get-tuple-element.247), channel_id=1, source_target_pairs={{1,0},{2,1},{3,2},{4,3},{5,4},{6,5},{7,6},{8,7},{9,8},{10,9},{11,1... | collective-permute-start | bytes 147464 | tf_op jit(solution)/shard_map/ppermute | solution.py:18
  31.2 6.6 %collective-permute-start.2 = (f32[3,2,1,4,4,128]{5,4,3,2,1,0:T(4,128)S(1)}, f32[3,2,1,4,4,128]{5,4,3,2,1,0:T(4,128)S(1)}, u32[]{:S(2)}, u32[]{:S(2)}) collective-permute-start(f32[3,2,1,4,4,128]{5,4,3,2,1,0:T(4,128)S(1)} %get-tuple-element.246), channel_id=1, source_target_pairs={{0,1},{1,2},{2,3},{3,4},{4,5},{5,6},{6,7},{7,8},{8,9},{9,10},{10,1... | collective-permute-start | bytes 147464 | tf_op jit(solution)/shard_map/ppermute | solution.py:17
  37.9 0.7 copy-start.2
  39.1 9.5 %collective-permute-start.5 = (f32[3,2,1,4,4,128]{5,4,3,2,1,0:T(4,128)S(1)}, f32[3,2,1,4,4,128]{5,4,3,2,1,0:T(4,128)S(1)}, u32[]{:S(2)}, u32[]{:S(2)}) collective-permute-start(f32[3,2,1,4,4,128]{5,4,3,2,1,0:T(4,128)S(1)} %get-tuple-element.245), channel_id=1, source_target_pairs={{1,0},{2,1},{3,2},{4,3},{5,4},{6,5},{7,6},{8,7},{9,8},{10,9},{11,1... | collective-permute-start | bytes 147464 | tf_op jit(solution)/shard_map/ppermute | solution.py:18
  40.4 8.2 %collective-permute-start.4 = (f32[3,2,1,4,4,128]{5,4,3,2,1,0:T(4,128)S(1)}, f32[3,2,1,4,4,128]{5,4,3,2,1,0:T(4,128)S(1)}, u32[]{:S(2)}, u32[]{:S(2)}) collective-permute-start(f32[3,2,1,4,4,128]{5,4,3,2,1,0:T(4,128)S(1)} %get-tuple-element.244), channel_id=1, source_target_pairs={{0,1},{1,2},{2,3},{3,4},{4,5},{5,6},{6,7},{7,8},{8,9},{9,10},{10,1... | collective-permute-start | bytes 147464 | tf_op jit(solution)/shard_map/ppermute | solution.py:17
  43.9 5.2 %collective-permute-start.12 = (f32[2,1,4,12,256]{4,2,3,1,0:T(4,128)S(1)}, f32[2,1,4,12,256]{4,2,3,1,0:T(4,128)S(1)}, u32[]{:S(2)}, u32[]{:S(2)}) collective-permute-start(f32[2,1,4,12,256]{4,2,3,1,0:T(4,128)S(1)} %get-tuple-element.190), channel_id=1, source_target_pairs={{0,1},{1,2},{2,3},{3,4},{4,5},{5,6},{6,7},{7,8},{8,9},{9,10},{10,1... | collective-permute-start | bytes 294920 | tf_op jit(solution)/shard_map/ppermute | solution.py:17
  47.3 3.2 collective-permute-start.13
  95.9 0.7 copy-start.10
  98.0 13.2 %all-to-all-start = ((f32[2,1,4,256]{2,0,1,3:T(2,128)}), f32[2,1,4,256]{2,0,1,3:T(2,128)S(1)}, u32[]{:S(2)}, u32[]{:S(2)}) async-start(f32[2,1,4,256]{2,0,1,3:T(2,128)} %copy.948), calls=%async_computation | async-start | bytes 524288 | tf_op jit(solution)/shard_map/all_to_all | solution.py:159
  101.8 27.1 %collective-permute-start.18 = (f32[2,1,4,12,256]{4,2,3,1,0:T(4,128)S(1)}, f32[2,1,4,12,256]{4,2,3,1,0:T(4,128)S(1)}, u32[]{:S(2)}, u32[]{:S(2)}) collective-permute-start(f32[2,1,4,12,256]{4,2,3,1,0:T(4,128)S(1)} %fusion.1100), channel_id=1, source_target_pairs={{1,0},{2,1},{3,2},{4,3},{5,4},{6,5},{7,6},{8,7},{9,8},{10,9},{11,1... | collective-permute-start | bytes 294920 | tf_op jit(solution)/shard_map/ppermute | solution.py:18
  103.1 25.8 %collective-permute-start.19 = (f32[2,1,4,12,256]{4,2,3,1,0:T(4,128)S(1)}, f32[2,1,4,12,256]{4,2,3,1,0:T(4,128)S(1)}, u32[]{:S(2)}, u32[]{:S(2)}) collective-permute-start(f32[2,1,4,12,256]{4,2,3,1,0:T(4,128)S(1)} %fusion.1100), channel_id=1, source_target_pairs={{0,1},{1,2},{2,3},{3,4},{4,5},{5,6},{6,7},{7,8},{8,9},{9,10},{10,1... | collective-permute-start | bytes 294920 | tf_op jit(solution)/shard_map/ppermute | solution.py:17
  112.7 10.8 %all-to-all-start.3 = ((f32[2,1,128,8]{3,0,1,2:T(2,128)}), f32[2,1,128,8]{3,0,1,2:T(2,128)S(1)}, u32[]{:S(2)}, u32[]{:S(2)}) async-start(f32[2,1,128,8]{3,0,1,2:T(2,128)} %copy.978), calls=%async_computation.3 | async-start | bytes 262144 | tf_op jit(solution)/shard_map/all_to_all | solution.py:131
  115.4 8.4 %collective-permute-start.7 = (f32[3,2,1,4,4,128]{5,4,3,2,1,0:T(4,128)S(1)}, f32[3,2,1,4,4,128]{5,4,3,2,1,0:T(4,128)S(1)}, u32[]{:S(2)}, u32[]{:S(2)}) collective-permute-start(f32[3,2,1,4,4,128]{5,4,3,2,1,0:T(4,128)S(1)} %get-tuple-element.243), channel_id=1, source_target_pairs={{1,0},{2,1},{3,2},{4,3},{5,4},{6,5},{7,6},{8,7},{9,8},{10,9},{11,1... | collective-permute-start | bytes 147464 | tf_op jit(solution)/shard_map/ppermute | solution.py:18
  116.7 7.2 %collective-permute-start.6 = (f32[3,2,1,4,4,128]{5,4,3,2,1,0:T(4,128)S(1)}, f32[3,2,1,4,4,128]{5,4,3,2,1,0:T(4,128)S(1)}, u32[]{:S(2)}, u32[]{:S(2)}) collective-permute-start(f32[3,2,1,4,4,128]{5,4,3,2,1,0:T(4,128)S(1)} %get-tuple-element.242), channel_id=1, source_target_pairs={{0,1},{1,2},{2,3},{3,4},{4,5},{5,6},{6,7},{7,8},{8,9},{9,10},{10,1... | collective-permute-start | bytes 147464 | tf_op jit(solution)/shard_map/ppermute | solution.py:17
  124.6 9.5 %collective-permute-start.9 = (f32[3,2,1,4,4,128]{5,4,3,2,1,0:T(4,128)S(1)}, f32[3,2,1,4,4,128]{5,4,3,2,1,0:T(4,128)S(1)}, u32[]{:S(2)}, u32[]{:S(2)}) collective-permute-start(f32[3,2,1,4,4,128]{5,4,3,2,1,0:T(4,128)S(1)} %get-tuple-element.241), channel_id=1, source_target_pairs={{1,0},{2,1},{3,2},{4,3},{5,4},{6,5},{7,6},{8,7},{9,8},{10,9},{11,1... | collective-permute-start | bytes 147464 | tf_op jit(solution)/shard_map/ppermute | solution.py:18
  125.9 8.2 %collective-permute-start.8 = (f32[3,2,1,4,4,128]{5,4,3,2,1,0:T(4,128)S(1)}, f32[3,2,1,4,4,128]{5,4,3,2,1,0:T(4,128)S(1)}, u32[]{:S(2)}, u32[]{:S(2)}) collective-permute-start(f32[3,2,1,4,4,128]{5,4,3,2,1,0:T(4,128)S(1)} %get-tuple-element.240), channel_id=1, source_target_pairs={{0,1},{1,2},{2,3},{3,4},{4,5},{5,6},{6,7},{7,8},{8,9},{9,10},{10,1... | collective-permute-start | bytes 147464 | tf_op jit(solution)/shard_map/ppermute | solution.py:17
  129.4 5.2 %collective-permute-start.20 = (f32[2,1,4,12,256]{4,2,3,1,0:T(4,128)S(1)}, f32[2,1,4,12,256]{4,2,3,1,0:T(4,128)S(1)}, u32[]{:S(2)}, u32[]{:S(2)}) collective-permute-start(f32[2,1,4,12,256]{4,2,3,1,0:T(4,128)S(1)} %get-tuple-element.220), channel_id=1, source_target_pairs={{0,1},{1,2},{2,3},{3,4},{4,5},{5,6},{6,7},{7,8},{8,9},{9,10},{10,1... | collective-permute-start | bytes 294920 | tf_op jit(solution)/shard_map/ppermute | solution.py:17
  132.8 3.2 collective-permute-start.21
  182.4 13.2 %all-to-all-start.2 = ((f32[2,1,4,256]{2,0,1,3:T(2,128)}), f32[2,1,4,256]{2,0,1,3:T(2,128)S(1)}, u32[]{:S(2)}, u32[]{:S(2)}) async-start(f32[2,1,4,256]{2,0,1,3:T(2,128)} %copy.966), calls=%async_computation.2 | async-start | bytes 524288 | tf_op jit(solution)/shard_map/all_to_all | solution.py:159
  186.2 27.1 %collective-permute-start.24 = (f32[2,1,4,12,256]{4,2,3,1,0:T(4,128)S(1)}, f32[2,1,4,12,256]{4,2,3,1,0:T(4,128)S(1)}, u32[]{:S(2)}, u32[]{:S(2)}) collective-permute-start(f32[2,1,4,12,256]{4,2,3,1,0:T(4,128)S(1)} %fusion.1101), channel_id=1, source_target_pairs={{1,0},{2,1},{3,2},{4,3},{5,4},{6,5},{7,6},{8,7},{9,8},{10,9},{11,1... | collective-permute-start | bytes 294920 | tf_op jit(solution)/shard_map/ppermute | solution.py:18
  187.5 25.8 %collective-permute-start.25 = (f32[2,1,4,12,256]{4,2,3,1,0:T(4,128)S(1)}, f32[2,1,4,12,256]{4,2,3,1,0:T(4,128)S(1)}, u32[]{:S(2)}, u32[]{:S(2)}) collective-permute-start(f32[2,1,4,12,256]{4,2,3,1,0:T(4,128)S(1)} %fusion.1101), channel_id=1, source_target_pairs={{0,1},{1,2},{2,3},{3,4},{4,5},{5,6},{6,7},{7,8},{8,9},{9,10},{10,1... | collective-permute-start | bytes 294920 | tf_op jit(solution)/shard_map/ppermute | solution.py:17
  197.1 10.8 %all-to-all-start.5 = ((f32[2,1,128,8]{3,0,1,2:T(2,128)}), f32[2,1,128,8]{3,0,1,2:T(2,128)S(1)}, u32[]{:S(2)}, u32[]{:S(2)}) async-start(f32[2,1,128,8]{3,0,1,2:T(2,128)} %copy.989), calls=%async_computation.5 | async-start | bytes 262144 | tf_op jit(solution)/shard_map/all_to_all | solution.py:131
  199.7 8.4 %collective-permute-start.15 = (f32[3,2,1,4,4,128]{5,4,3,2,1,0:T(4,128)S(1)}, f32[3,2,1,4,4,128]{5,4,3,2,1,0:T(4,128)S(1)}, u32[]{:S(2)}, u32[]{:S(2)}) collective-permute-start(f32[3,2,1,4,4,128]{5,4,3,2,1,0:T(4,128)S(1)} %get-tuple-element.239), channel_id=1, source_target_pairs={{1,0},{2,1},{3,2},{4,3},{5,4},{6,5},{7,6},{8,7},{9,8},{10,9},{11,1... | collective-permute-start | bytes 147464 | tf_op jit(solution)/shard_map/ppermute | solution.py:18
  201.0 7.2 %collective-permute-start.14 = (f32[3,2,1,4,4,128]{5,4,3,2,1,0:T(4,128)S(1)}, f32[3,2,1,4,4,128]{5,4,3,2,1,0:T(4,128)S(1)}, u32[]{:S(2)}, u32[]{:S(2)}) collective-permute-start(f32[3,2,1,4,4,128]{5,4,3,2,1,0:T(4,128)S(1)} %get-tuple-element.238), channel_id=1, source_target_pairs={{0,1},{1,2},{2,3},{3,4},{4,5},{5,6},{6,7},{7,8},{8,9},{9,10},{10,1... | collective-permute-start | bytes 147464 | tf_op jit(solution)/shard_map/ppermute | solution.py:17
  209.0 9.5 %collective-permute-start.17 = (f32[3,2,1,4,4,128]{5,4,3,2,1,0:T(4,128)S(1)}, f32[3,2,1,4,4,128]{5,4,3,2,1,0:T(4,128)S(1)}, u32[]{:S(2)}, u32[]{:S(2)}) collective-permute-start(f32[3,2,1,4,4,128]{5,4,3,2,1,0:T(4,128)S(1)} %get-tuple-element.237), channel_id=1, source_target_pairs={{1,0},{2,1},{3,2},{4,3},{5,4},{6,5},{7,6},{8,7},{9,8},{10,9},{11,1... | collective-permute-start | bytes 147464 | tf_op jit(solution)/shard_map/ppermute | solution.py:18
  210.3 8.2 %collective-permute-start.16 = (f32[3,2,1,4,4,128]{5,4,3,2,1,0:T(4,128)S(1)}, f32[3,2,1,4,4,128]{5,4,3,2,1,0:T(4,128)S(1)}, u32[]{:S(2)}, u32[]{:S(2)}) collective-permute-start(f32[3,2,1,4,4,128]{5,4,3,2,1,0:T(4,128)S(1)} %get-tuple-element.236), channel_id=1, source_target_pairs={{0,1},{1,2},{2,3},{3,4},{4,5},{5,6},{6,7},{7,8},{8,9},{9,10},{10,1... | collective-permute-start | bytes 147464 | tf_op jit(solution)/shard_map/ppermute | solution.py:17
  213.8 5.2 %collective-permute-start.26 = (f32[2,1,4,12,256]{4,2,3,1,0:T(4,128)S(1)}, f32[2,1,4,12,256]{4,2,3,1,0:T(4,128)S(1)}, u32[]{:S(2)}, u32[]{:S(2)}) collective-permute-start(f32[2,1,4,12,256]{4,2,3,1,0:T(4,128)S(1)} %get-tuple-element.212), channel_id=1, source_target_pairs={{0,1},{1,2},{2,3},{3,4},{4,5},{5,6},{6,7},{7,8},{8,9},{9,10},{10,1... | collective-permute-start | bytes 294920 | tf_op jit(solution)/shard_map/ppermute | solution.py:17
  217.2 3.2 collective-permute-start.27
  266.8 13.2 %all-to-all-start.4 = ((f32[2,1,4,256]{2,0,1,3:T(2,128)}), f32[2,1,4,256]{2,0,1,3:T(2,128)S(1)}, u32[]{:S(2)}, u32[]{:S(2)}) async-start(f32[2,1,4,256]{2,0,1,3:T(2,128)} %copy.981), calls=%async_computation.4 | async-start | bytes 524288 | tf_op jit(solution)/shard_map/all_to_all | solution.py:159
  270.6 23.3 %collective-permute-start.28 = (f32[2,1,4,12,256]{4,2,3,1,0:T(4,128)S(1)}, f32[2,1,4,12,256]{4,2,3,1,0:T(4,128)S(1)}, u32[]{:S(2)}, u32[]{:S(2)}) collective-permute-start(f32[2,1,4,12,256]{4,2,3,1,0:T(4,128)S(1)} %fusion.1102), channel_id=1, source_target_pairs={{1,0},{2,1},{3,2},{4,3},{5,4},{6,5},{7,6},{8,7},{9,8},{10,9},{11,1... | collective-permute-start | bytes 294920 | tf_op jit(solution)/shard_map/ppermute | solution.py:18
  271.9 22.0 %collective-permute-start.29 = (f32[2,1,4,12,256]{4,2,3,1,0:T(4,128)S(1)}, f32[2,1,4,12,256]{4,2,3,1,0:T(4,128)S(1)}, u32[]{:S(2)}, u32[]{:S(2)}) collective-permute-start(f32[2,1,4,12,256]{4,2,3,1,0:T(4,128)S(1)} %fusion.1102), channel_id=1, source_target_pairs={{0,1},{1,2},{2,3},{3,4},{4,5},{5,6},{6,7},{7,8},{8,9},{9,10},{10,1... | collective-permute-start | bytes 294920 | tf_op jit(solution)/shard_map/ppermute | solution.py:17
  281.5 10.8 %all-to-all-start.6 = ((f32[2,1,128,8]{3,0,1,2:T(2,128)}), f32[2,1,128,8]{3,0,1,2:T(2,128)S(1)}, u32[]{:S(2)}, u32[]{:S(2)}) async-start(f32[2,1,128,8]{3,0,1,2:T(2,128)} %copy.992), calls=%async_computation.6 | async-start | bytes 262144 | tf_op jit(solution)/shard_map/all_to_all | solution.py:131
  284.1 8.4 %collective-permute-start.23 = (f32[3,2,1,4,4,128]{5,4,3,2,1,0:T(4,128)S(1)}, f32[3,2,1,4,4,128]{5,4,3,2,1,0:T(4,128)S(1)}, u32[]{:S(2)}, u32[]{:S(2)}) collective-permute-start(f32[3,2,1,4,4,128]{5,4,3,2,1,0:T(4,128)S(1)} %get-tuple-element.235), channel_id=1, source_target_pairs={{1,0},{2,1},{3,2},{4,3},{5,4},{6,5},{7,6},{8,7},{9,8},{10,9},{11,1... | collective-permute-start | bytes 147464 | tf_op jit(solution)/shard_map/ppermute | solution.py:18
  285.4 7.2 %collective-permute-start.22 = (f32[3,2,1,4,4,128]{5,4,3,2,1,0:T(4,128)S(1)}, f32[3,2,1,4,4,128]{5,4,3,2,1,0:T(4,128)S(1)}, u32[]{:S(2)}, u32[]{:S(2)}) collective-permute-start(f32[3,2,1,4,4,128]{5,4,3,2,1,0:T(4,128)S(1)} %get-tuple-element.234), channel_id=1, source_target_pairs={{0,1},{1,2},{2,3},{3,4},{4,5},{5,6},{6,7},{7,8},{8,9},{9,10},{10,1... | collective-permute-start | bytes 147464 | tf_op jit(solution)/shard_map/ppermute | solution.py:17
  294.4 4.1 %collective-permute-start.30 = (f32[2,1,4,12,256]{4,2,3,1,0:T(4,128)S(1)}, f32[2,1,4,12,256]{4,2,3,1,0:T(4,128)S(1)}, u32[]{:S(2)}, u32[]{:S(2)}) collective-permute-start(f32[2,1,4,12,256]{4,2,3,1,0:T(4,128)S(1)} %get-tuple-element.204), channel_id=1, source_target_pairs={{0,1},{1,2},{2,3},{3,4},{4,5},{5,6},{6,7},{7,8},{8,9},{9,10},{10,1... | collective-permute-start | bytes 294920 | tf_op jit(solution)/shard_map/ppermute | solution.py:17
  296.5 3.9 %collective-permute-start.31 = (f32[2,1,4,12,256]{4,2,3,1,0:T(4,128)S(1)}, f32[2,1,4,12,256]{4,2,3,1,0:T(4,128)S(1)}, u32[]{:S(2)}, u32[]{:S(2)}) collective-permute-start(f32[2,1,4,12,256]{4,2,3,1,0:T(4,128)S(1)} %get-tuple-element.204), channel_id=1, source_target_pairs={{1,0},{2,1},{3,2},{4,3},{5,4},{6,5},{7,6},{8,7},{9,8},{10,9},{11,1... | collective-permute-start | bytes 294920 | tf_op jit(solution)/shard_map/ppermute | solution.py:18
  (2 other events, 1.3 us)
